TPU v7x, 32 devices: a whole 2x2x4 slice. The times are simulated.
32 devices in a mesh: seq: 8 (over z, x), exp: 4 (over y, core).
Axes of the slice: x: 2, y: 2, z: 4, core: 2. Of those that a mesh axis runs over, the one named last changes fastest.
Arguments:
- hidden_in: bfloat16 [2048, 1536], P('seq'), may hold values from -6 to 6
- attn_gain: float32 [1536], replicated, may hold values from 0.1 to 1.9
- q_weight: bfloat16 [1536, 1536], P(None, 'exp'), may hold values from -1.25 to 1.25
- k_weight: bfloat16 [1536, 512], P(None, 'exp'), may hold values from -0.625 to 0.625
- v_weight: bfloat16 [1536, 512], P(None, 'exp'), may hold values from -0.15625 to 0.15625
- o_weight: bfloat16 [1536, 1536], P('exp'), may hold values from -0.15625 to 0.15625
- cache_kv: bfloat16 [4096, 1024], P('seq', 'exp'), may hold values from -216 to 216
- moe_gain: float32 [1536], replicated, may hold values from 0.1 to 1.9
- expert_in: bfloat16 [32, 1536, 1024], P('seq'), may hold values from -0.15625 to 0.15625
- expert_out: bfloat16 [32, 512, 1536], P('seq'), may hold values from -0.25 to 0.25
- routes: int32 [2048, 8], P(('seq', 'exp')), may hold values from 0 to 31, all different within a row; in each aligned block of 64 rows (0 to 63, 64 to 127, ...) at most 32 rows name the same one
- route_prob: float32 [2048, 8], P(('seq', 'exp')), may hold values from 0.05 to 1
- page_slot: int32 [256], replicated, may hold values from 0 to 31, as said below
Outputs:
- hidden_out: bfloat16 [2048, 1536], P(('seq', 'exp'))
- decode_pages: bfloat16 [256, 8, 2, 512], P('seq', 'exp')
Inputs may be any that keep to these rules, and one draw needn't show every extreme that they name: `routes`: in each aligned block of 64 rows (the rows of one device) no expert is named by more than 32 rows; a row names 8 different experts. `page_slot`: for each r, the 32 blocks b with b mod (8) == r have different slots.
All inputs are finite; a program needn't handle non-finite values.
Results may differ from a plain program's by a relative error of at most 0.0074.
Values may be sent and summed in bfloat16 or wider, within the bound.
No kernel may reach another device: no remote copies, remote signals or barrier semaphores. Data moves between devices by JAX's collectives and lax.ppermute only.
A program may use at most 128 MiB of HBM per device.

v0:
```python
import math
import jax
import jax.numpy as jnp
from jax import lax
from jax.sharding import PartitionSpec as P

HEADS = 24
KV_HEADS = 8
HEAD_DIM = 64
EXPERTS = 32
PAGE = 8
norm_epsilon = 1e-06
attention_scale = 0.015625
residual_scale = 0.22
masked_score = -1e30


def rms_norm(values, gain_row):
    widened = values.astype(jnp.float32)
    spread = lax.rsqrt(jnp.mean(widened * widened, axis=-1, keepdims=True) + norm_epsilon)
    return (widened * spread * gain_row).astype(jnp.bfloat16)


def attend_block(carried, query_heads, visible, key_rows, value_rows):
    best_old, total_old, summed_old = carried
    scores = (
        jnp.einsum("tkgd,nkd->kgtn", query_heads, key_rows, preferred_element_type=jnp.float32)
        * attention_scale
    )
    scores = jnp.where(visible, scores, masked_score)
    best_new = jnp.maximum(best_old, jnp.max(scores, axis=-1))
    weights = jnp.where(visible, jnp.exp(scores - best_new[..., None]), 0.0)
    factor = jnp.exp(best_old - best_new)
    total_new = total_old * factor + jnp.sum(weights, axis=-1)
    summed_new = summed_old * factor[..., None] + jnp.einsum(
        "kgtn,nkd->kgtd",
        weights.astype(jnp.bfloat16),
        value_rows,
        preferred_element_type=jnp.float32,
    )
    return (best_new, total_new, summed_new)


def block_size(piece_rows):
    return math.gcd(piece_rows, 512)


def body(
    hidden_in,
    attn_gain,
    q_weight,
    k_weight,
    v_weight,
    o_weight,
    cache_kv,
    moe_gain,
    expert_in,
    expert_out,
    routes,
    route_prob,
    page_slot,
):
    seq_count = lax.axis_size("seq")
    seq_index = lax.axis_index("seq")
    exp_index = lax.axis_index("exp")
    tokens_here = hidden_in.shape[0]
    head_dim = HEAD_DIM
    kv_local = k_weight.shape[1] // head_dim
    group_size = HEADS // KV_HEADS
    prompt_len = tokens_here * seq_count // 2
    first_row = seq_index * tokens_here
    query_rows = first_row + jnp.arange(tokens_here, dtype=jnp.int32)
    query_second = query_rows >= prompt_len
    holds_first = first_row < prompt_len
    normed = rms_norm(hidden_in, attn_gain)
    queries = jnp.dot(normed, q_weight, preferred_element_type=jnp.float32).astype(jnp.bfloat16)
    keys_new = jnp.dot(normed, k_weight, preferred_element_type=jnp.float32).astype(jnp.bfloat16)
    values_new = jnp.dot(normed, v_weight, preferred_element_type=jnp.float32).astype(jnp.bfloat16)
    pair_width = 2 * kv_local * head_dim
    pairs_new = jnp.stack(
        [
            keys_new.reshape(tokens_here, kv_local, head_dim),
            values_new.reshape(tokens_here, kv_local, head_dim),
        ],
        axis=2,
    ).reshape(tokens_here, pair_width)
    query_heads = queries.reshape(tokens_here, kv_local, group_size, head_dim)
    cache_lines = cache_kv.reshape(tokens_here, -1)
    blocks_here = tokens_here // PAGE
    rounds = blocks_here // seq_count
    outgoing = pairs_new.reshape(rounds, seq_count, PAGE * pair_width)
    received = lax.all_to_all(outgoing, "seq", split_axis=1, concat_axis=1, tiled=True)
    block_ids = (
        jnp.arange(seq_count, dtype=jnp.int32)[None, :] * blocks_here
        + jnp.arange(rounds, dtype=jnp.int32)[:, None] * seq_count
        + seq_index
    ).reshape(-1)
    table_ids = jnp.arange(page_slot.shape[0], dtype=jnp.int32)
    page_slots = jnp.sum(
        jnp.where(block_ids[:, None] == table_ids[None, :], page_slot[None, :], 0), axis=1
    )
    local_pages = (
        jnp.zeros((blocks_here, PAGE * pair_width), jnp.bfloat16)
        .at[page_slots]
        .set(received.reshape(blocks_here, -1))
    )
    page_rows = local_pages.reshape(blocks_here, PAGE, kv_local, 2, head_dim).transpose(
        0, 2, 3, 1, 4
    )
    page_rows = page_rows.reshape(blocks_here, kv_local, 2, PAGE * head_dim)
    start_state = (
        jnp.full((kv_local, group_size, tokens_here), masked_score, jnp.float32),
        jnp.zeros((kv_local, group_size, tokens_here), jnp.float32),
        jnp.zeros((kv_local, group_size, tokens_here, head_dim), jnp.float32),
    )

    def new_keys_part(carried, new_block, key_first):
        width_rows = new_block.shape[0]
        key_rows = key_first + jnp.arange(width_rows, dtype=jnp.int32)
        visible = ((key_rows >= prompt_len)[None, :] == query_second[:, None]) & (
            key_rows[None, :] <= query_rows[:, None]
        )
        split_pairs = new_block.reshape(width_rows, kv_local, 2, head_dim)
        return lax.cond(
            jnp.any(visible),
            lambda carried_in: attend_block(
                carried_in, query_heads, visible, split_pairs[:, :, 0], split_pairs[:, :, 1]
            ),
            lambda carried_in: carried_in,
            carried,
        )

    carried = start_state
    new_piece = lax.all_gather(pairs_new, "seq", axis=0, tiled=True)
    cache_piece = lax.all_gather(cache_lines, "seq", axis=0, tiled=True)
    piece_rows = new_piece.shape[0]
    stride = block_size(piece_rows)
    new_blocks = new_piece.reshape(piece_rows // stride, stride, -1)
    cache_blocks = cache_piece.reshape(piece_rows // stride, 2 * stride, kv_local, 2, head_dim)
    offsets = stride * jnp.arange(piece_rows // stride, dtype=jnp.int32)
    everything = jnp.ones((tokens_here, 2 * stride), bool)

    def visit(carried_in, block_part):
        new_block, cache_block, key_first = block_part
        carried_in = new_keys_part(carried_in, new_block, key_first)
        carried_in = lax.cond(
            holds_first,
            lambda inner: attend_block(
                inner, query_heads, everything, cache_block[:, :, 0], cache_block[:, :, 1]
            ),
            lambda inner: inner,
            carried_in,
        )
        return (carried_in, None)

    carried, _ = lax.scan(visit, carried, (new_blocks, cache_blocks, offsets))
    best_final, total_final, summed_final = carried
    attended = (
        (summed_final / total_final[..., None])
        .transpose(2, 0, 1, 3)
        .reshape(tokens_here, -1)
        .astype(jnp.bfloat16)
    )
    mixed_rows = lax.psum_scatter(
        jnp.dot(attended, o_weight, preferred_element_type=jnp.float32).astype(jnp.bfloat16),
        "exp",
        scatter_dimension=0,
        tiled=True,
    ).astype(jnp.float32)
    moe_rows = mixed_rows.shape[0]
    residual = (
        lax.dynamic_slice_in_dim(hidden_in, exp_index * moe_rows, moe_rows, 0).astype(jnp.float32)
        + residual_scale * mixed_rows
    )
    moe_in = rms_norm(residual, moe_gain)
    top_count = routes.shape[1]
    assigns = moe_rows * top_count
    capacity = 2 * moe_rows * top_count // EXPERTS
    flat_ids = routes.reshape(-1)
    hit_table = (flat_ids[:, None] == jnp.arange(EXPERTS, dtype=jnp.int32)[None, :]).astype(
        jnp.int32
    )
    earlier = jnp.cumsum(hit_table, axis=0) - hit_table
    slot_rank = jnp.sum(earlier * hit_table, axis=1)
    dest_slot = flat_ids * capacity + slot_rank
    source = (
        jnp.full((EXPERTS * capacity,), assigns, jnp.int32)
        .at[dest_slot]
        .set(jnp.arange(assigns, dtype=jnp.int32))
    )
    filled = source < assigns
    picked = moe_in[jnp.minimum(source, assigns - 1) // top_count]
    dispatched = jnp.where(filled[:, None], picked, jnp.zeros_like(picked)).reshape(
        seq_count, EXPERTS // seq_count, capacity, -1
    )
    hidden = jnp.einsum(
        "sexd,edf->sexf",
        lax.all_to_all(dispatched, "seq", split_axis=0, concat_axis=0, tiled=True),
        expert_in,
        preferred_element_type=jnp.float32,
    )
    half_width = hidden.shape[-1] // 2
    active = (jax.nn.silu(hidden[..., :half_width]) * hidden[..., half_width:]).astype(jnp.bfloat16)
    produced = jnp.einsum(
        "sexf,efd->sexd", active, expert_out, preferred_element_type=jnp.float32
    ).astype(jnp.bfloat16)
    returned = lax.all_to_all(produced, "seq", split_axis=0, concat_axis=0, tiled=True)
    flat_back = returned.reshape(EXPERTS * capacity, -1)
    per_assign = flat_back[dest_slot].reshape(moe_rows, top_count, -1)
    share = route_prob / jnp.sum(route_prob, axis=-1, keepdims=True)
    moe = jnp.sum(share[..., None] * per_assign.astype(jnp.float32), axis=1)
    hidden_out = (residual + residual_scale * moe).astype(jnp.bfloat16)
    return (hidden_out, page_rows)


def solution(mesh):
    return jax.shard_map(
        body,
        mesh=mesh,
        in_specs=(
            P("seq", None),
            P(),
            P(None, "exp"),
            P(None, "exp"),
            P(None, "exp"),
            P("exp", None),
            P("seq", "exp"),
            P(),
            P("seq", None, None),
            P("seq", None, None),
            P(("seq", "exp"), None),
            P(("seq", "exp"), None),
            P(),
        ),
        out_specs=(P(("seq", "exp"), None), P("seq", "exp", None, None)),
        check_vma=False,
    )
```

profile of v0, /device:TPU:0, one launch (start us, length us, event | category | flops | bytes accessed | tf_op | source)
XLA Modules:
  0.0 385.0 jit_solution(13722507623709581729)
XLA Ops:
  7.3 1.5 fusion.45
  8.8 1.7 convolution_convert_fusion.3
  10.5 1.7 convolution_convert_fusion.2
  14.7 40.6 %all-gather.3.cloned.1.call-done = bf16[2048,256]{0,1:T(8,128)(2,1)} async-done(((bf16[256,256]{0,1:T(8,128)(2,1)}), bf16[2048,256]{0,1:T(8,128)(2,1)}) %all-gather.3.cloned.1.call-update) | async-done | bytes 1048592 | tf_op jit(solution)/shard_map/all_gather | solution.py:134
  55.4 1.3 copy.142
  56.7 49.0 %all-gather.5.cloned.1.call-done = bf16[2048,512]{1,0:T(8,128)(2,1)} async-done(((bf16[256,512]{1,0:T(8,128)(2,1)}), bf16[2048,512]{1,0:T(8,128)(2,1)}) %all-gather.5.cloned.1.call-update) | async-done | bytes 2097168 | tf_op jit(solution)/shard_map/all_gather | solution.py:135
  105.7 8.9 %reshape.173 = bf16[4,1024,2,2,64]{4,3,2,1,0:T(2,128)(2,1)} reshape(bf16[2048,512]{1,0:T(8,128)(2,1)} %all-gather.5.cloned.1.call-done) | data formatting | bytes 4194304 | tf_op jit(solution)/shard_map/reshape | solution.py:139
  114.6 10.6 %copy.101 = bf16[4,1024,2,2,64]{1,4,2,3,0:T(8,128)(2,1)} copy(bf16[4,1024,2,2,64]{4,3,2,1,0:T(2,128)(2,1)} %reshape.173) | data formatting | bytes 4194304
  125.3 35.4 %while.16 = (s32[]{:T(128)}, f32[2,3,256]{2,1,0:T(4,128)S(1)}, f32[2,3,256]{2,1,0:T(4,128)S(1)}, f32[2,3,256,64]{2,3,1,0:T(8,128)S(1)}, pred[]{:T(512)}, /*index...) while((s32[]{:T(128)}, f32[2,3,256]{2,1,0:T(4,128)S(1)}, ...), condition=%wide.region_11.12_spmd.clone.clone, body=%wide.region_1.11_spmd.clone.clone.sunk | while | flops 627712256 | bytes 33374036 | solution.py:156
  129.0 2.5 conditional.8
  131.5 4.5 %conditional.9 = ((f32[2,3,256]{2,1,0:T(4,128)S(1)}, f32[2,3,256]{2,1,0:T(4,128)S(1)}, f32[2,3,256,64]{2,3,1,0:T(8,128)S(1)})) conditional(s32[]{:T(128)} %convert_element_type.152, (f32[2,3,256]{2,1,0:T(4,128)S(1)}, f32[2,3,256]{2,1,0:T(4,128)S(1)}, f32[2,3,256,64]{2,3,1,0:T(8,128)S(1)}) %get-tuple-element.445, ...), branch_computations={%region_7.7_spmd, %region_8.10_spmd} | conditional | flops 415435776 | bytes 21532708 | solution.py:146
  139.7 4.5 %conditional.9 = ((f32[2,3,256]{2,1,0:T(4,128)S(1)}, f32[2,3,256]{2,1,0:T(4,128)S(1)}, f32[2,3,256,64]{2,3,1,0:T(8,128)S(1)})) conditional(s32[]{:T(128)} %convert_element_type.152, (f32[2,3,256]{2,1,0:T(4,128)S(1)}, f32[2,3,256]{2,1,0:T(4,128)S(1)}, f32[2,3,256,64]{2,3,1,0:T(8,128)S(1)}) %get-tuple-element.445, ...), branch_computations={%region_7.7_spmd, %region_8.10_spmd} | conditional | flops 415435776 | bytes 21532708 | solution.py:146
  143.0 1.2 fusion.22
  148.0 4.5 %conditional.9 = ((f32[2,3,256]{2,1,0:T(4,128)S(1)}, f32[2,3,256]{2,1,0:T(4,128)S(1)}, f32[2,3,256,64]{2,3,1,0:T(8,128)S(1)})) conditional(s32[]{:T(128)} %convert_element_type.152, (f32[2,3,256]{2,1,0:T(4,128)S(1)}, f32[2,3,256]{2,1,0:T(4,128)S(1)}, f32[2,3,256,64]{2,3,1,0:T(8,128)S(1)}) %get-tuple-element.445, ...), branch_computations={%region_7.7_spmd, %region_8.10_spmd} | conditional | flops 415435776 | bytes 21532708 | solution.py:146
  151.2 1.2 fusion.22
  156.2 4.5 %conditional.9 = ((f32[2,3,256]{2,1,0:T(4,128)S(1)}, f32[2,3,256]{2,1,0:T(4,128)S(1)}, f32[2,3,256,64]{2,3,1,0:T(8,128)S(1)})) conditional(s32[]{:T(128)} %convert_element_type.152, (f32[2,3,256]{2,1,0:T(4,128)S(1)}, f32[2,3,256]{2,1,0:T(4,128)S(1)}, f32[2,3,256,64]{2,3,1,0:T(8,128)S(1)}) %get-tuple-element.445, ...), branch_computations={%region_7.7_spmd, %region_8.10_spmd} | conditional | flops 415435776 | bytes 21532708 | solution.py:146
  160.8 1.5 convolution_convert_fusion
  164.3 2.4 scatter_custom_fusion
  166.9 19.4 %reduce-scatter.2.cloned.1.call-done = bf16[64,1536]{1,0:T(8,128)(2,1)} async-done(((bf16[256,1536]{1,0:T(8,128)(2,1)}), bf16[64,1536]{1,0:T(8,128)(2,1)}) %reduce-scatter.2.cloned.1.call-update) | async-done | bytes 196624 | tf_op jit(solution)/shard_map/reduce_scatter | solution.py:164
  188.5 5.6 %gather_fusion = bf16[1024,1536]{1,0:T(8,128)(2,1)} fusion(bf16[64,1536]{1,0:T(8,128)(2,1)S(1)} %multiply_convert_fusion, s32[1024]{0:T(1024)S(1)} %fusion.59), kind=kCustom, calls=%fused_computation | custom fusion | bytes 6295552 | tf_op jit(solution)/shard_map/gather | solution.py:192
  194.1 3.8 broadcast_select_fusion
  197.9 5.8 %all-to-all-start = ((bf16[8,4,32,1536]{3,2,1,0:T(8,128)(2,1)}), bf16[8,4,32,1536]{3,2,1,0:T(8,128)(2,1)}, u32[]{:S(2)}, u32[]{:S(2)}) async-start(bf16[8,4,32,1536]{3,2,1,0:T(8,128)(2,1)} %broadcast_select_fusion), calls=%async_computation.1 | async-start | bytes 6291456 | tf_op jit(solution)/shard_map/all_to_all | solution.py:198
  204.9 69.6 %all-to-all-done = bf16[8,4,32,1536]{3,2,1,0:T(8,128)(2,1)} async-done(((bf16[8,4,32,1536]{3,2,1,0:T(8,128)(2,1)}), bf16[8,4,32,1536]{3,2,1,0:T(8,128)(2,1)}, u32[]{:S(2)}, u32[]{:S(2)}) %all-to-all-start) | async-done | bytes 3145760 | tf_op jit(solution)/shard_map/all_to_all | solution.py:198
  274.5 3.6 all-to-all-start.2
  278.2 7.4 %fusion.39 = f32[8,4,32,1024]{3,2,0,1:T(8,128)S(1)} fusion(bf16[4,1536,1024]{2,1,0:T(8,128)(2,1)} %param.27, bf16[8,4,32,1536]{3,2,1,0:T(8,128)(2,1)} %all-to-all-done), kind=kOutput, calls=%fused_computation.53 | convolution fusion | flops 3221225472 | bytes 19922944 | tf_op jit(solution)/shard_map/sexd,edf->sexf/dot_general | solution.py:196
  285.6 4.6 %fusion.34 = bf16[8,4,32,1536]{3,2,0,1:T(8,128)(2,1)S(1)} fusion(bf16[4,512,1536]{2,1,0:T(8,128)(2,1)} %param.28, f32[8,4,32,1024]{3,2,0,1:T(8,128)S(1)} %fusion.39), kind=kOutput, calls=%fused_computation.47 | convolution fusion | flops 1615331328 | bytes 13631488 | tf_op jit(solution)/shard_map/sexf,efd->sexd/dot_general | solution.py:204
  290.2 1.9 copy.108
  292.1 6.1 %all-to-all-start.1 = ((bf16[8,4,32,1536]{3,2,1,0:T(8,128)(2,1)}), bf16[8,4,32,1536]{3,2,1,0:T(8,128)(2,1)}, u32[]{:S(2)}, u32[]{:S(2)}) async-start(bf16[8,4,32,1536]{3,2,1,0:T(8,128)(2,1)} %copy.108), calls=%async_computation.2 | async-start | bytes 6291456 | tf_op jit(solution)/shard_map/all_to_all | solution.py:207
  301.4 67.3 %all-to-all-done.1 = bf16[8,4,32,1536]{3,2,1,0:T(8,128)(2,1)} async-done(((bf16[8,4,32,1536]{3,2,1,0:T(8,128)(2,1)}), bf16[8,4,32,1536]{3,2,1,0:T(8,128)(2,1)}, u32[]{:S(2)}, u32[]{:S(2)}) %all-to-all-start.1) | async-done | bytes 3145760 | tf_op jit(solution)/shard_map/all_to_all | solution.py:207
  368.7 5.9 %gather_fusion.1 = bf16[512,1536]{1,0:T(8,128)(2,1)S(1)} fusion(bf16[1024,1536]{1,0:T(8,128)(2,1)} %bitcast.33, s32[1024]{0:T(1024)S(1)} %pad_clamp_fusion), kind=kCustom, calls=%fused_computation.1 | custom fusion | bytes 3147776 | tf_op jit(solution)/shard_map/gather | solution.py:209
  374.6 2.2 fusion.37
  376.8 1.7 add_convert_fusion
  (139 shorter events, 40.8 us)
Async XLA Ops:
  7.2 153.6 %copy-start = (bf16[384,1536]{1,0:T(8,128)(2,1)S(1)}, bf16[384,1536]{1,0:T(8,128)(2,1)}, u32[]{:S(2)}) copy-start(bf16[384,1536]{1,0:T(8,128)(2,1)} %param.24) | copy-start | bytes 3538948
  7.2 6.7 %copy-start.1 = (bf16[256,1536]{1,0:T(8,128)(2,1)S(1)}, bf16[256,1536]{1,0:T(8,128)(2,1)}, u32[]{:S(2)}) copy-start(bf16[256,1536]{1,0:T(8,128)(2,1)} %param.19) | copy-start | bytes 2359300
  7.2 6.7 %copy-start.10 = (f32[1536]{0:T(1024)S(1)}, f32[1536]{0:T(1024)}, u32[]{:S(2)}) copy-start(f32[1536]{0:T(1024)} %param.20) | copy-start | bytes 18436
  7.2 5.8 %copy-start.4 = (bf16[512,256]{1,0:T(8,128)(2,1)S(1)}, bf16[512,256]{1,0:T(8,128)(2,1)}, u32[]{:S(2)}) copy-start(bf16[512,256]{1,0:T(8,128)(2,1)} %param.25) | copy-start | bytes 786436
  7.2 6.7 %copy-start.9 = (bf16[1536,384]{1,0:T(8,128)(2,1)S(1)}, bf16[1536,384]{1,0:T(8,128)(2,1)}, u32[]{:S(2)}) copy-start(bf16[1536,384]{1,0:T(8,128)(2,1)} %param.21) | copy-start | bytes 3538948
  7.2 48.1 %all-gather.3.cloned.1.call-start = ((), (), s32[]{:S(2)}) async-start(), calls=%async_computation.4 | async-start | bytes 1179648 | tf_op jit(solution)/shard_map/all_gather | solution.py:134
  13.0 92.7 %all-gather.5.cloned.1.call-start = ((), (), s32[]{:S(2)}) async-start(), calls=%async_computation.5 | async-start | bytes 2359296 | tf_op jit(solution)/shard_map/all_gather | solution.py:135
  13.9 172.4 %reduce-scatter.2.cloned.1.call-start = ((), (), s32[]{:S(2)}) async-start(), calls=%async_computation.6 | async-start | bytes 983040 | tf_op jit(solution)/shard_map/reduce_scatter | solution.py:164
  160.7 1.6 copy-start.5
  160.7 25.6 %copy-start.2 = (bf16[256,1536]{1,0:T(8,128)(2,1)S(1)}, bf16[256,1536]{1,0:T(8,128)(2,1)}, u32[]{:S(2)}) copy-start(bf16[256,1536]{1,0:T(8,128)(2,1)} %param.19) | copy-start | bytes 2359300
  160.7 26.7 %copy-start.7 = (f32[1536]{0:T(1024)S(1)}, f32[1536]{0:T(1024)}, u32[]{:S(2)}) copy-start(f32[1536]{0:T(1024)} %param.26) | copy-start | bytes 18436
  197.9 5.8 %copy-start.3 = (bf16[256,2,2,64]{0,3,2,1:T(8,128)(2,1)S(1)}, bf16[256,2,2,64]{0,3,2,1:T(8,128)(2,1)}, u32[]{:S(2)}) copy-start(bf16[256,2,2,64]{0,3,2,1:T(8,128)(2,1)} %pad_maximum_fusion) | copy-start | bytes 393220
  197.9 76.6 %all-to-all-start = ((bf16[8,4,32,1536]{3,2,1,0:T(8,128)(2,1)}), bf16[8,4,32,1536]{3,2,1,0:T(8,128)(2,1)}, u32[]{:S(2)}, u32[]{:S(2)}) async-start(bf16[8,4,32,1536]{3,2,1,0:T(8,128)(2,1)} %broadcast_select_fusion), calls=%async_computation.1 | async-start | bytes 6291456 | tf_op jit(solution)/shard_map/all_to_all | solution.py:198
  274.5 17.6 %all-to-all-start.2 = ((bf16[4,8,2048]{2,0,1:T(4,128)(2,1)}), bf16[4,8,2048]{2,0,1:T(4,128)(2,1)S(1)}, u32[]{:S(2)}, u32[]{:S(2)}) async-start(bf16[4,8,2048]{2,0,1:T(4,128)(2,1)} %copy.110), calls=%async_computation.3 | async-start | bytes 262144 | tf_op jit(solution)/shard_map/all_to_all | solution.py:92
  292.1 6.1 %copy-start.6 = (f32[64,8]{0,1:T(8,128)S(1)}, f32[64,8]{0,1:T(8,128)}, u32[]{:S(2)}) copy-start(f32[64,8]{0,1:T(8,128)} %param.30) | copy-start | bytes 6148
  292.1 7.1 %copy-start.8 = (s32[256]{0:T(256)S(1)}, s32[256]{0:T(256)}, u32[]{:S(2)}) copy-start(s32[256]{0:T(256)} %param.31) | copy-start | bytes 3076
  292.1 76.6 %all-to-all-start.1 = ((bf16[8,4,32,1536]{3,2,1,0:T(8,128)(2,1)}), bf16[8,4,32,1536]{3,2,1,0:T(8,128)(2,1)}, u32[]{:S(2)}, u32[]{:S(2)}) async-start(bf16[8,4,32,1536]{3,2,1,0:T(8,128)(2,1)} %copy.108), calls=%async_computation.2 | async-start | bytes 6291456 | tf_op jit(solution)/shard_map/all_to_all | solution.py:207
Sparse Core Ops, SparseCore 0:
  13.1 42.2 all-gather.2
  57.5 48.1 all-gather.4
  162.4 23.8 reduce-scatter.1
where the time goes:
time: 386 us; the launch traced here: 385 us
  waiting for transfers between devices  246 us (64%)
  local copies, waits for them, and re-layouts  49.6 us (13%)
  matrix products  28.3 us (7%)
  other arithmetic  28.1 us (7%)
  starting transfers between devices  15.7 us (4%)
  between operations  14.1 us (4%)
    all_to_all x1, waiting for transfers between devices, body(): lax.all_to_all(dispatched, 'seq', split_axis=0, concat_axis=0, tiled=True)  69.6 us
    all_to_all x1, waiting for transfers between devices, body(): lax.all_to_all(produced, 'seq', split_axis=0, concat_axis=0, tiled=True)  67.3 us
    all_gather x1, waiting for transfers between devices, body(): cache_piece = lax.all_gather(cache_lines, 'seq', axis=0, tiled=True)  49 us
    all_gather x1, waiting for transfers between devices, body(): new_piece = lax.all_gather(pairs_new, 'seq', axis=0, tiled=True)  40.6 us
    reduce_scatter x1, waiting for transfers between devices, body(): lax.psum_scatter(jnp.dot(attended, o_weight, preferred_element_type=jnp.f...  19.4 us
    unnamed x26, local copies, waits for them, and re-layouts  11.7 us
    reshape x1, local copies, waits for them, and re-layouts, body(): cache_piece.reshape(piece_rows // stride, 2 * stride, kv_local, 2, head_dim)  8.88 us
  transfers between devices with their start and end apart: 6, of which 5 were waited for; matrix products, arithmetic and copies ran while one was open for 7% of the time, Pallas kernels for 0%

commit v1 on v0

--- a/solution.py
+++ b/solution.py
@@ -3,6 +3,7 @@
 import jax.numpy as jnp
 from jax import lax
 from jax.sharding import PartitionSpec as P
+from jax.lax import axis_index, axis_size, ppermute
 
 HEADS = 24
 KV_HEADS = 8
@@ -13,6 +14,14 @@
 attention_scale = 0.015625
 residual_scale = 0.22
 masked_score = -1e30
+
+
+def zone_cut(state, dim_at):
+    state = jnp.moveaxis(state, 0, dim_at)
+    piece_now = state.shape
+    return state.reshape(
+        *piece_now[:dim_at], piece_now[dim_at] * piece_now[dim_at + 1], *piece_now[dim_at + 2 :]
+    )
 
 
 def rms_norm(values, gain_row):
@@ -132,7 +141,18 @@
 
     carried = start_state
     new_piece = lax.all_gather(pairs_new, "seq", axis=0, tiled=True)
-    cache_piece = lax.all_gather(cache_lines, "seq", axis=0, tiled=True)
+
+    def expand_the_bench(s0, axis_name, k_dim):
+        cores_n = axis_size(axis_name)
+        in_order = list(map(lambda d: (d, (d + 1) % cores_n), range(cores_n)))
+        views = [s0]
+        while len(views) < cores_n:
+            views.append(ppermute(views[-1], axis_name, in_order))
+        block_next = axis_index(axis_name)
+        views = jnp.stack(views)[(block_next - jnp.arange(cores_n)) % cores_n]
+        return zone_cut(views, k_dim)
+
+    cache_piece = expand_the_bench(cache_lines, "seq", k_dim=0)
     piece_rows = new_piece.shape[0]
     stride = block_size(piece_rows)
     new_blocks = new_piece.reshape(piece_rows // stride, stride, -1)

time: 386 us -> 358 us (0.927)
  waiting for transfers between devices: 246 us -> 212 us
    ppermute x0 -> x7, waiting for transfers between devices: none -> 59 us  [expand_the_bench(): views.append(ppermute(views[-1], axis_name, in_order))]
    all_gather x1 -> x0, waiting for transfers between devices: 49 us -> none  [body(): cache_piece = lax.all_gather(cache_lines, 'seq', axis=0, tiled=True)]
    all_gather x1, waiting for transfers between devices: 40.6 us -> 0.01 us  [body(): new_piece = lax.all_gather(pairs_new, 'seq', axis=0, tiled=True)]
    reshape x1 -> x0, local copies, waits for them, and re-layouts: 8.88 us -> none  [body(): cache_piece.reshape(piece_rows // stride, 2 * stride, kv_local, 2, head_dim)]
    unnamed x26 -> x31, local copies, waits for them, and re-layouts: 11.7 us -> 16.7 us
    another operation x1 -> x4, local copies, waits for them, and re-layouts: 0.01 us -> 4.48 us  [the longest x1 3.66 us: body(): cache_piece.reshape(piece_rows // stride, 2 * stride, kv_local, 2, head_dim)]
  transfers between devices with their start and end apart: 6 -> 12, of which waited for: 5 -> 10; matrix products, arithmetic and copies ran while one was open for 7% -> 15% of each run, Pallas kernels for 0% -> 0%
where the time goes in v1:
time: 358 us; the launch traced here: 356 us
  waiting for transfers between devices  212 us (59%)
  local copies, waits for them, and re-layouts  52.7 us (15%)
  matrix products  29.6 us (8%)
  other arithmetic  26.7 us (7%)
  starting transfers between devices  18.5 us (5%)
  between operations  14.4 us (4%)
    all_to_all x1, waiting for transfers between devices, body(): lax.all_to_all(dispatched, 'seq', split_axis=0, concat_axis=0, tiled=True)  69.6 us
    all_to_all x1, waiting for transfers between devices, body(): lax.all_to_all(produced, 'seq', split_axis=0, concat_axis=0, tiled=True)  67.3 us
    ppermute x7, waiting for transfers between devices, expand_the_bench(): views.append(ppermute(views[-1], axis_name, in_order))  59 us
    unnamed x31, local copies, waits for them, and re-layouts  16.7 us
    reduce_scatter x1, waiting for transfers between devices, body(): lax.psum_scatter(jnp.dot(attended, o_weight, preferred_element_type=jnp.f...  15.8 us
    dot_general x1, matrix products, body(): jnp.einsum('sexd,edf->sexf', lax.all_to_all(dispatched, 'seq', split_axis...  7.37 us
  transfers between devices with their start and end apart: 12, of which 10 were waited for; matrix products, arithmetic and copies ran while one was open for 15% of the time, Pallas kernels for 0%

profile of v1, /device:TPU:0, one launch (start us, length us, event | category | flops | bytes accessed | tf_op | source)
XLA Modules:
  0.0 356.5 jit_solution(16678271732345256377)
XLA Ops:
  8.4 3.0 collective-permute-start
  14.6 6.2 %collective-permute-done = bf16[256,512]{1,0:T(8,128)(2,1)S(1)} collective-permute-done((bf16[256,512]{1,0:T(8,128)(2,1)S(1)}, bf16[256,512]{1,0:T(8,128)(2,1)S(1)}, u32[]{:S(2)}, u32[]{:S(2)}) %collective-permute-start) | collective-permute-done | bytes 262176 | tf_op jit(solution)/shard_map/ppermute | solution.py:150
  23.3 7.7 %collective-permute-done.1 = bf16[256,512]{1,0:T(8,128)(2,1)S(1)} collective-permute-done((bf16[256,512]{1,0:T(8,128)(2,1)S(1)}, bf16[256,512]{1,0:T(8,128)(2,1)S(1)}, u32[]{:S(2)}, u32[]{:S(2)}) %collective-permute-start.1) | collective-permute-done | bytes 262176 | tf_op jit(solution)/shard_map/ppermute | solution.py:150
  31.0 1.9 convolution_convert_fusion.1
  32.9 8.9 %collective-permute-done.2 = bf16[256,512]{1,0:T(8,128)(2,1)S(1)} collective-permute-done((bf16[256,512]{1,0:T(8,128)(2,1)S(1)}, bf16[256,512]{1,0:T(8,128)(2,1)S(1)}, u32[]{:S(2)}, u32[]{:S(2)}) %collective-permute-start.2) | collective-permute-done | bytes 262176 | tf_op jit(solution)/shard_map/ppermute | solution.py:150
  42.8 8.1 %collective-permute-done.3 = bf16[256,512]{1,0:T(8,128)(2,1)S(1)} collective-permute-done((bf16[256,512]{1,0:T(8,128)(2,1)S(1)}, bf16[256,512]{1,0:T(8,128)(2,1)S(1)}, u32[]{:S(2)}, u32[]{:S(2)}) %collective-permute-start.3) | collective-permute-done | bytes 262176 | tf_op jit(solution)/shard_map/ppermute | solution.py:150
  52.3 13.0 %collective-permute-done.4 = bf16[256,512]{1,0:T(8,128)(2,1)S(1)} collective-permute-done((bf16[256,512]{1,0:T(8,128)(2,1)S(1)}, bf16[256,512]{1,0:T(8,128)(2,1)S(1)}, u32[]{:S(2)}, u32[]{:S(2)}) %collective-permute-start.4) | collective-permute-done | bytes 262176 | tf_op jit(solution)/shard_map/ppermute | solution.py:150
  66.7 7.6 %collective-permute-done.5 = bf16[256,512]{1,0:T(8,128)(2,1)S(1)} collective-permute-done((bf16[256,512]{1,0:T(8,128)(2,1)S(1)}, bf16[256,512]{1,0:T(8,128)(2,1)S(1)}, u32[]{:S(2)}, u32[]{:S(2)}) %collective-permute-start.5) | collective-permute-done | bytes 262176 | tf_op jit(solution)/shard_map/ppermute | solution.py:150
  75.8 7.6 %collective-permute-done.6 = bf16[256,512]{1,0:T(8,128)(2,1)S(1)} collective-permute-done((bf16[256,512]{1,0:T(8,128)(2,1)S(1)}, bf16[256,512]{1,0:T(8,128)(2,1)S(1)}, u32[]{:S(2)}, u32[]{:S(2)}) %collective-permute-start.6) | collective-permute-done | bytes 262176 | tf_op jit(solution)/shard_map/ppermute | solution.py:150
  84.1 2.3 gather_fusion
  86.4 3.7 %reshape_reshape.6 = bf16[4,1024,2,2,64]{4,3,2,1,0:T(2,128)(2,1)} reshape(bf16[8,256,512]{2,1,0:T(8,128)(2,1)S(1)} %gather_fusion) | data formatting | bytes 4194304 | tf_op jit(solution)/shard_map/reshape;reshape | solution.py:159
  90.0 10.6 %copy.101 = bf16[4,1024,2,2,64]{1,4,2,3,0:T(8,128)(2,1)} copy(bf16[4,1024,2,2,64]{4,3,2,1,0:T(2,128)(2,1)} %reshape_reshape.6) | data formatting | bytes 4194304
  102.1 33.4 %while.16 = (s32[]{:T(128)}, f32[2,3,256]{2,1,0:T(4,128)S(1)}, f32[2,3,256]{2,1,0:T(4,128)S(1)}, f32[2,3,256,64]{2,3,1,0:T(8,128)S(1)}, pred[]{:T(512)}, /*index...) while((s32[]{:T(128)}, f32[2,3,256]{2,1,0:T(4,128)S(1)}, ...), condition=%wide.region_11.12_spmd.clone.clone, body=%wide.region_1.11_spmd.clone.clone.sunk | while | flops 627712256 | bytes 33374036 | solution.py:176
  105.3 2.5 conditional.8
  107.8 4.5 %conditional.9 = ((f32[2,3,256]{2,1,0:T(4,128)S(1)}, f32[2,3,256]{2,1,0:T(4,128)S(1)}, f32[2,3,256,64]{2,3,1,0:T(8,128)S(1)})) conditional(s32[]{:T(128)} %convert_element_type.152, (f32[2,3,256]{2,1,0:T(4,128)S(1)}, f32[2,3,256]{2,1,0:T(4,128)S(1)}, f32[2,3,256,64]{2,3,1,0:T(8,128)S(1)}) %get-tuple-element.445, ...), branch_computations={%region_7.7_spmd, %region_8.10_spmd} | conditional | flops 415435776 | bytes 21532708 | solution.py:166
  115.5 4.5 %conditional.9 = ((f32[2,3,256]{2,1,0:T(4,128)S(1)}, f32[2,3,256]{2,1,0:T(4,128)S(1)}, f32[2,3,256,64]{2,3,1,0:T(8,128)S(1)})) conditional(s32[]{:T(128)} %convert_element_type.152, (f32[2,3,256]{2,1,0:T(4,128)S(1)}, f32[2,3,256]{2,1,0:T(4,128)S(1)}, f32[2,3,256,64]{2,3,1,0:T(8,128)S(1)}) %get-tuple-element.445, ...), branch_computations={%region_7.7_spmd, %region_8.10_spmd} | conditional | flops 415435776 | bytes 21532708 | solution.py:166
  123.3 4.5 %conditional.9 = ((f32[2,3,256]{2,1,0:T(4,128)S(1)}, f32[2,3,256]{2,1,0:T(4,128)S(1)}, f32[2,3,256,64]{2,3,1,0:T(8,128)S(1)})) conditional(s32[]{:T(128)} %convert_element_type.152, (f32[2,3,256]{2,1,0:T(4,128)S(1)}, f32[2,3,256]{2,1,0:T(4,128)S(1)}, f32[2,3,256,64]{2,3,1,0:T(8,128)S(1)}) %get-tuple-element.445, ...), branch_computations={%region_7.7_spmd, %region_8.10_spmd} | conditional | flops 415435776 | bytes 21532708 | solution.py:166
  131.0 4.5 %conditional.9 = ((f32[2,3,256]{2,1,0:T(4,128)S(1)}, f32[2,3,256]{2,1,0:T(4,128)S(1)}, f32[2,3,256,64]{2,3,1,0:T(8,128)S(1)})) conditional(s32[]{:T(128)} %convert_element_type.152, (f32[2,3,256]{2,1,0:T(4,128)S(1)}, f32[2,3,256]{2,1,0:T(4,128)S(1)}, f32[2,3,256,64]{2,3,1,0:T(8,128)S(1)}) %get-tuple-element.445, ...), branch_computations={%region_7.7_spmd, %region_8.10_spmd} | conditional | flops 415435776 | bytes 21532708 | solution.py:166
  139.1 2.6 scatter_custom_fusion
  141.9 15.8 %reduce-scatter.2.cloned.1.call-done = bf16[64,1536]{1,0:T(8,128)(2,1)} async-done(((bf16[256,1536]{1,0:T(8,128)(2,1)}), bf16[64,1536]{1,0:T(8,128)(2,1)}) %reduce-scatter.2.cloned.1.call-update) | async-done | bytes 196624 | tf_op jit(solution)/shard_map/reduce_scatter | solution.py:184
  159.8 5.6 %gather_fusion.1 = bf16[1024,1536]{1,0:T(8,128)(2,1)} fusion(bf16[64,1536]{1,0:T(8,128)(2,1)S(1)} %multiply_convert_fusion, s32[1024]{0:T(1024)S(1)} %fusion.59), kind=kCustom, calls=%fused_computation.1 | custom fusion | bytes 6295552 | tf_op jit(solution)/shard_map/gather | solution.py:212
  165.4 3.8 %broadcast_select_fusion = bf16[8,4,32,1536]{3,2,1,0:T(8,128)(2,1)} fusion(bf16[8,4,32,1536]{3,2,1,0:T(8,128)(2,1)} %bitcast.157, pred[8,4,32]{2,1,0:T(4,128)(4,1)S(1)} %broadcast_in_dim.87), kind=kLoop, calls=%fused_computation.52 | loop fusion | flops 1572864 | bytes 6292480 | tf_op jit(solution)/shard_map/jit(_where)/select_n | solution.py:213
  169.2 5.6 %all-to-all-start = ((bf16[8,4,32,1536]{3,2,1,0:T(8,128)(2,1)}), bf16[8,4,32,1536]{3,2,1,0:T(8,128)(2,1)}, u32[]{:S(2)}, u32[]{:S(2)}) async-start(bf16[8,4,32,1536]{3,2,1,0:T(8,128)(2,1)} %broadcast_select_fusion), calls=%async_computation.1 | async-start | bytes 6291456 | tf_op jit(solution)/shard_map/all_to_all | solution.py:218
  176.1 69.6 %all-to-all-done = bf16[8,4,32,1536]{3,2,1,0:T(8,128)(2,1)} async-done(((bf16[8,4,32,1536]{3,2,1,0:T(8,128)(2,1)}), bf16[8,4,32,1536]{3,2,1,0:T(8,128)(2,1)}, u32[]{:S(2)}, u32[]{:S(2)}) %all-to-all-start) | async-done | bytes 3145760 | tf_op jit(solution)/shard_map/all_to_all | solution.py:218
  245.7 3.6 %all-to-all-start.2 = ((bf16[4,8,2048]{2,0,1:T(4,128)(2,1)}), bf16[4,8,2048]{2,0,1:T(4,128)(2,1)S(1)}, u32[]{:S(2)}, u32[]{:S(2)}) async-start(bf16[4,8,2048]{2,0,1:T(4,128)(2,1)} %copy.110), calls=%async_computation.3 | async-start | bytes 262144 | tf_op jit(solution)/shard_map/all_to_all | solution.py:101
  249.3 7.4 %fusion.39 = f32[8,4,32,1024]{3,2,0,1:T(8,128)S(1)} fusion(bf16[4,1536,1024]{2,1,0:T(8,128)(2,1)} %param.27, bf16[8,4,32,1536]{3,2,1,0:T(8,128)(2,1)} %all-to-all-done), kind=kOutput, calls=%fused_computation.54 | convolution fusion | flops 3221225472 | bytes 19922944 | tf_op jit(solution)/shard_map/sexd,edf->sexf/dot_general | solution.py:216
  256.7 4.6 %fusion.34 = bf16[8,4,32,1536]{3,2,0,1:T(8,128)(2,1)S(1)} fusion(bf16[4,512,1536]{2,1,0:T(8,128)(2,1)} %param.28, f32[8,4,32,1024]{3,2,0,1:T(8,128)S(1)} %fusion.39), kind=kOutput, calls=%fused_computation.48 | convolution fusion | flops 1615331328 | bytes 13631488 | tf_op jit(solution)/shard_map/sexf,efd->sexd/dot_general | solution.py:224
  261.3 1.9 copy.108
  263.3 6.1 %all-to-all-start.1 = ((bf16[8,4,32,1536]{3,2,1,0:T(8,128)(2,1)}), bf16[8,4,32,1536]{3,2,1,0:T(8,128)(2,1)}, u32[]{:S(2)}, u32[]{:S(2)}) async-start(bf16[8,4,32,1536]{3,2,1,0:T(8,128)(2,1)} %copy.108), calls=%async_computation.2 | async-start | bytes 6291456 | tf_op jit(solution)/shard_map/all_to_all | solution.py:227
  272.5 67.3 %all-to-all-done.1 = bf16[8,4,32,1536]{3,2,1,0:T(8,128)(2,1)} async-done(((bf16[8,4,32,1536]{3,2,1,0:T(8,128)(2,1)}), bf16[8,4,32,1536]{3,2,1,0:T(8,128)(2,1)}, u32[]{:S(2)}, u32[]{:S(2)}) %all-to-all-start.1) | async-done | bytes 3145760 | tf_op jit(solution)/shard_map/all_to_all | solution.py:227
  339.8 5.9 %gather_fusion.2 = bf16[512,1536]{1,0:T(8,128)(2,1)S(1)} fusion(bf16[1024,1536]{1,0:T(8,128)(2,1)} %bitcast.41, s32[1024]{0:T(1024)S(1)} %pad_clamp_fusion), kind=kCustom, calls=%fused_computation.2 | custom fusion | bytes 3147776 | tf_op jit(solution)/shard_map/gather | solution.py:229
  345.7 2.2 fusion.37
  (160 shorter events, 56.7 us)
Async XLA Ops:
  7.2 128.4 %copy-start = (bf16[384,1536]{1,0:T(8,128)(2,1)S(1)}, bf16[384,1536]{1,0:T(8,128)(2,1)}, u32[]{:S(2)}) copy-start(bf16[384,1536]{1,0:T(8,128)(2,1)} %param.24) | copy-start | bytes 3538948
  7.2 23.8 %copy-start.1 = (bf16[256,1536]{1,0:T(8,128)(2,1)S(1)}, bf16[256,1536]{1,0:T(8,128)(2,1)}, u32[]{:S(2)}) copy-start(bf16[256,1536]{1,0:T(8,128)(2,1)} %param.19) | copy-start | bytes 2359300
  7.2 23.8 %copy-start.9 = (f32[1536]{0:T(1024)S(1)}, f32[1536]{0:T(1024)}, u32[]{:S(2)}) copy-start(f32[1536]{0:T(1024)} %param.20) | copy-start | bytes 18436
  7.2 93.5 %all-gather.2.cloned.1.call-start = ((), (), s32[]{:S(2)}) async-start(), calls=%async_computation.4 | async-start | bytes 1179648 | tf_op jit(solution)/shard_map/all_gather | solution.py:143
  8.4 12.3 %collective-permute-start = (bf16[256,512]{1,0:T(8,128)(2,1)S(1)}, bf16[256,512]{1,0:T(8,128)(2,1)S(1)}, u32[]{:S(2)}, u32[]{:S(2)}) collective-permute-start(bf16[256,512]{1,0:T(8,128)(2,1)S(1)} %reshape.218), channel_id=1, source_target_pairs={{0,4},{4,8},{8,12},{12,16},{16,20},{20,24},{24,28},{28,0},{1,5},{5... | collective-permute-start | bytes 786440 | tf_op jit(solution)/shard_map/ppermute | solution.py:150
  12.8 29.0 %copy-start.4 = (bf16[512,256]{1,0:T(8,128)(2,1)S(1)}, bf16[512,256]{1,0:T(8,128)(2,1)}, u32[]{:S(2)}) copy-start(bf16[512,256]{1,0:T(8,128)(2,1)} %param.25) | copy-start | bytes 786436
  20.8 10.2 %collective-permute-start.1 = (bf16[256,512]{1,0:T(8,128)(2,1)S(1)}, bf16[256,512]{1,0:T(8,128)(2,1)S(1)}, u32[]{:S(2)}, u32[]{:S(2)}) collective-permute-start(bf16[256,512]{1,0:T(8,128)(2,1)S(1)} %collective-permute-done), channel_id=1, source_target_pairs={{0,4},{4,8},{8,12},{12,16},{16,20},{20,24},{24,28},{28,0},{1,5},{5... | collective-permute-start | bytes 786440 | tf_op jit(solution)/shard_map/ppermute | solution.py:150
  23.2 134.4 %reduce-scatter.2.cloned.1.call-start = ((), (), s32[]{:S(2)}) async-start(), calls=%async_computation.5 | async-start | bytes 983040 | tf_op jit(solution)/shard_map/reduce_scatter | solution.py:184
  30.9 10.8 %collective-permute-start.2 = (bf16[256,512]{1,0:T(8,128)(2,1)S(1)}, bf16[256,512]{1,0:T(8,128)(2,1)S(1)}, u32[]{:S(2)}, u32[]{:S(2)}) collective-permute-start(bf16[256,512]{1,0:T(8,128)(2,1)S(1)} %collective-permute-done.1), channel_id=1, source_target_pairs={{0,4},{4,8},{8,12},{12,16},{16,20},{20,24},{24,28},{28,0},{1,5},{5... | collective-permute-start | bytes 786440 | tf_op jit(solution)/shard_map/ppermute | solution.py:150
  41.8 9.1 %collective-permute-start.3 = (bf16[256,512]{1,0:T(8,128)(2,1)S(1)}, bf16[256,512]{1,0:T(8,128)(2,1)S(1)}, u32[]{:S(2)}, u32[]{:S(2)}) collective-permute-start(bf16[256,512]{1,0:T(8,128)(2,1)S(1)} %collective-permute-done.2), channel_id=1, source_target_pairs={{0,4},{4,8},{8,12},{12,16},{16,20},{20,24},{24,28},{28,0},{1,5},{5... | collective-permute-start | bytes 786440 | tf_op jit(solution)/shard_map/ppermute | solution.py:150
  50.8 14.4 %collective-permute-start.4 = (bf16[256,512]{1,0:T(8,128)(2,1)S(1)}, bf16[256,512]{1,0:T(8,128)(2,1)S(1)}, u32[]{:S(2)}, u32[]{:S(2)}) collective-permute-start(bf16[256,512]{1,0:T(8,128)(2,1)S(1)} %collective-permute-done.3), channel_id=1, source_target_pairs={{0,4},{4,8},{8,12},{12,16},{16,20},{20,24},{24,28},{28,0},{1,5},{5... | collective-permute-start | bytes 786440 | tf_op jit(solution)/shard_map/ppermute | solution.py:150
  65.2 9.1 %collective-permute-start.5 = (bf16[256,512]{1,0:T(8,128)(2,1)S(1)}, bf16[256,512]{1,0:T(8,128)(2,1)S(1)}, u32[]{:S(2)}, u32[]{:S(2)}) collective-permute-start(bf16[256,512]{1,0:T(8,128)(2,1)S(1)} %collective-permute-done.4), channel_id=1, source_target_pairs={{0,4},{4,8},{8,12},{12,16},{16,20},{20,24},{24,28},{28,0},{1,5},{5... | collective-permute-start | bytes 786440 | tf_op jit(solution)/shard_map/ppermute | solution.py:150
  74.3 9.1 %collective-permute-start.6 = (bf16[256,512]{1,0:T(8,128)(2,1)S(1)}, bf16[256,512]{1,0:T(8,128)(2,1)S(1)}, u32[]{:S(2)}, u32[]{:S(2)}) collective-permute-start(bf16[256,512]{1,0:T(8,128)(2,1)S(1)} %collective-permute-done.5), channel_id=1, source_target_pairs={{0,4},{4,8},{8,12},{12,16},{16,20},{20,24},{24,28},{28,0},{1,5},{5... | collective-permute-start | bytes 786440 | tf_op jit(solution)/shard_map/ppermute | solution.py:150
  135.5 1.6 copy-start.5
  135.5 22.1 %copy-start.2 = (bf16[256,1536]{1,0:T(8,128)(2,1)S(1)}, bf16[256,1536]{1,0:T(8,128)(2,1)}, u32[]{:S(2)}) copy-start(bf16[256,1536]{1,0:T(8,128)(2,1)} %param.19) | copy-start | bytes 2359300
  135.5 23.2 %copy-start.7 = (f32[1536]{0:T(1024)S(1)}, f32[1536]{0:T(1024)}, u32[]{:S(2)}) copy-start(f32[1536]{0:T(1024)} %param.26) | copy-start | bytes 18436
  169.2 5.6 %copy-start.3 = (bf16[256,2,2,64]{0,3,2,1:T(8,128)(2,1)S(1)}, bf16[256,2,2,64]{0,3,2,1:T(8,128)(2,1)}, u32[]{:S(2)}) copy-start(bf16[256,2,2,64]{0,3,2,1:T(8,128)(2,1)} %pad_maximum_fusion) | copy-start | bytes 393220
  169.2 76.5 %all-to-all-start = ((bf16[8,4,32,1536]{3,2,1,0:T(8,128)(2,1)}), bf16[8,4,32,1536]{3,2,1,0:T(8,128)(2,1)}, u32[]{:S(2)}, u32[]{:S(2)}) async-start(bf16[8,4,32,1536]{3,2,1,0:T(8,128)(2,1)} %broadcast_select_fusion), calls=%async_computation.1 | async-start | bytes 6291456 | tf_op jit(solution)/shard_map/all_to_all | solution.py:218
  245.7 17.6 %all-to-all-start.2 = ((bf16[4,8,2048]{2,0,1:T(4,128)(2,1)}), bf16[4,8,2048]{2,0,1:T(4,128)(2,1)S(1)}, u32[]{:S(2)}, u32[]{:S(2)}) async-start(bf16[4,8,2048]{2,0,1:T(4,128)(2,1)} %copy.110), calls=%async_computation.3 | async-start | bytes 262144 | tf_op jit(solution)/shard_map/all_to_all | solution.py:101
  263.3 6.1 %copy-start.6 = (f32[64,8]{0,1:T(8,128)S(1)}, f32[64,8]{0,1:T(8,128)}, u32[]{:S(2)}) copy-start(f32[64,8]{0,1:T(8,128)} %param.30) | copy-start | bytes 6148
  263.3 7.0 %copy-start.8 = (s32[256]{0:T(256)S(1)}, s32[256]{0:T(256)}, u32[]{:S(2)}) copy-start(s32[256]{0:T(256)} %param.31) | copy-start | bytes 3076
  263.3 76.6 %all-to-all-start.1 = ((bf16[8,4,32,1536]{3,2,1,0:T(8,128)(2,1)}), bf16[8,4,32,1536]{3,2,1,0:T(8,128)(2,1)}, u32[]{:S(2)}, u32[]{:S(2)}) async-start(bf16[8,4,32,1536]{3,2,1,0:T(8,128)(2,1)} %copy.108), calls=%async_computation.2 | async-start | bytes 6291456 | tf_op jit(solution)/shard_map/all_to_all | solution.py:227
Sparse Core Ops, SparseCore 0:
  23.3 47.4 all-gather.1
  137.2 20.3 reduce-scatter.1
